TPU v7x, 128 devices: a whole 4x4x4 slice. The times are simulated.
128 devices in a mesh: rep: 4 (over z), node: 4 (over y), local: 8 (over x, core).
Axes of the slice: x: 4, y: 4, z: 4, core: 2. Of those that a mesh axis runs over, the one named last changes fastest.
Arguments:
- tokens: bfloat16 [8192, 7168], P(('rep', 'node', 'local')), parts along dimension 0, may hold values from -6 to 6
- expert_ids: int32 [8192, 8], P(('rep', 'node', 'local')), parts along dimension 0, may hold values from 0 to 127, as said below
- node_groups: int32 [8192, 2], P(('rep', 'node', 'local')), parts along dimension 0, may hold values from 0 to 3, as said below
- gate_levels: int32 [8192, 8], P(('rep', 'node', 'local')), parts along dimension 0, may hold values from 1 to 255
- expert_seeds: int32 [128], P(('node', 'local')), may hold values from 0 to 999999999
Outputs:
- routed_out: bfloat16 [8192, 7168], P(('rep', 'node', 'local')), parts along dimension 0
There are 4 independent parts, one for each index of `rep`. A program takes and returns all parts, laid end to end along the dimension named above; an argument that names none is the same for every part. Nothing has to cross between parts.
Inputs may be any that keep to these rules, and one draw needn't show every extreme that they name: `expert_ids`: each row names 8 different experts; expert e belongs to node group e // 32. `node_groups`: each row names 2 different node groups.
All inputs are finite; a program needn't handle non-finite values.
Results may differ from a plain program's by a relative error of at most 0.0085.
Values may be sent and summed in bfloat16 or wider, within the bound.
No kernel may reach another device: no remote copies, remote signals or barrier semaphores. Data moves between devices by JAX's collectives and lax.ppermute only.
A program may use at most 192 MiB of HBM per device.

v0:
```python
import math

import jax
import jax.numpy as jnp
from jax import lax
from jax.sharding import PartitionSpec as P

D = 7168
FF = 1024
TOP = 8
EXP_DEV = 4


route_scale = 2.5
salt_gate = 1013904223
salt_up = 1664525
salt_down = 22695477


def hashed_weight(expert_seed, salt_value, row_count, column_count, fan_in):
    row_index = lax.broadcasted_iota(jnp.int32, (row_count, column_count), 0)
    column_index = lax.broadcasted_iota(jnp.int32, (row_count, column_count), 1)
    hashed = (
        (row_index * column_count + column_index) * 747796405
        + expert_seed * 1103515245
        + salt_value
    )
    hashed = hashed ^ hashed >> 15
    hashed = hashed * 277803737
    hashed = hashed ^ hashed >> 13
    hashed = hashed * 668265263
    hashed = hashed ^ hashed >> 16
    sixteen_bits = (hashed >> 8 & 65535).astype(jnp.float32)
    return ((sixteen_bits - 32767.5) * (math.sqrt(3.0 / fan_in) / 32768.0)).astype(jnp.bfloat16)


def expert_block(block_rows, expert_seed):
    weight_gate = hashed_weight(expert_seed, salt_gate, D, FF, D)
    weight_up = hashed_weight(expert_seed, salt_up, D, FF, D)
    weight_down = hashed_weight(expert_seed, salt_down, FF, D, FF)
    gate_part = jnp.dot(block_rows, weight_gate, preferred_element_type=jnp.float32)
    up_part = jnp.dot(block_rows, weight_up, preferred_element_type=jnp.float32)
    hidden = (jax.nn.silu(gate_part) * up_part).astype(jnp.bfloat16)
    return jnp.dot(hidden, weight_down, preferred_element_type=jnp.float32).astype(jnp.bfloat16)


def run_experts(expert_rows, local_seeds):

    def per_expert(running, scan_item):
        expert_seed, block_rows = scan_item
        return (running, expert_block(block_rows, expert_seed))

    unused, outputs = lax.scan(per_expert, jnp.zeros((), jnp.int32), (local_seeds, expert_rows))
    return outputs


def group_mask(expert_ids, node_groups, group_size):
    return jnp.any((expert_ids // group_size)[:, :, None] == node_groups[:, None, :], axis=2)


def gate_of(gate_levels, in_group):
    levels = gate_levels.astype(jnp.float32)
    return (
        route_scale * levels * in_group.astype(jnp.float32) / jnp.sum(levels, axis=1, keepdims=True)
    )


def rank_of(expert_ids, in_group, blocks, capacity, experts_total):
    expert_range = jnp.arange(experts_total, dtype=jnp.int32)
    hit_table = (
        (expert_ids[:, :, None] == expert_range[None, None, :]) & in_group[:, :, None]
    ).astype(jnp.int32)
    present = jnp.sum(hit_table, axis=1, dtype=jnp.int32)
    blocked = present.reshape(blocks, -1, experts_total)
    before = (jnp.cumsum(blocked, axis=1, dtype=jnp.int32) - blocked).reshape(-1, experts_total)
    slot_rank = jnp.sum(hit_table * before[:, None, :], axis=2, dtype=jnp.int32)
    kept_mask = in_group & (slot_rank < capacity)
    return (slot_rank, kept_mask)


def fill_slots(row_block, slot_index, slot_total):
    row_count = row_block.shape[0]
    token_index = lax.broadcasted_iota(jnp.int32, slot_index.shape, 0)
    slot_token = (
        jnp.full((slot_total,), row_count, jnp.int32)
        .at[slot_index.reshape(-1)]
        .set(token_index.reshape(-1), mode="drop")
    )
    padded = jnp.concatenate(
        [row_block, jnp.zeros((1, row_block.shape[1]), row_block.dtype)], axis=0
    )
    return padded[slot_token]


def combine_rows(returned, slot_index, gate_share):
    padded = jnp.concatenate([returned, jnp.zeros((1, returned.shape[1]), returned.dtype)], axis=0)
    picked = padded[slot_index]
    return jnp.einsum("tj,tjd->td", gate_share, picked.astype(jnp.float32))


def on_device(tokens, expert_ids, node_groups, gate_levels, expert_seeds):
    tok_count = tokens.shape[0]
    width = tokens.shape[1]
    devices_all = lax.axis_size(("node", "local"))
    local_count = lax.axis_size("local")
    experts_total = EXP_DEV * devices_all
    capacity = max(2, tok_count * TOP // experts_total)
    group_size = EXP_DEV * local_count
    in_group = group_mask(expert_ids, node_groups, group_size)
    gate_share = gate_of(gate_levels, in_group)
    slot_rank, kept_mask = rank_of(expert_ids, in_group, 1, capacity, experts_total)
    slot_total = experts_total * capacity
    slot_index = jnp.where(kept_mask, expert_ids * capacity + slot_rank, slot_total)
    send_rows = fill_slots(tokens, slot_index, slot_total).reshape(
        devices_all, EXP_DEV, capacity, width
    )
    arrived = lax.all_to_all(send_rows, ("node", "local"), split_axis=0, concat_axis=2, tiled=True)
    results = run_experts(arrived.reshape(EXP_DEV, -1, width), expert_seeds)
    returned = lax.all_to_all(
        results.reshape(1, EXP_DEV, -1, width),
        ("node", "local"),
        split_axis=2,
        concat_axis=0,
        tiled=True,
    )
    return combine_rows(returned.reshape(slot_total, width), slot_index, gate_share).astype(
        jnp.bfloat16
    )


def solution(mesh):
    in_specs = (
        P(("rep", "node", "local"), None),
        P(("rep", "node", "local"), None),
        P(("rep", "node", "local"), None),
        P(("rep", "node", "local"), None),
        P(("node", "local")),
    )
    out_specs = P(("rep", "node", "local"), None)
    return jax.shard_map(
        on_device, mesh=mesh, in_specs=in_specs, out_specs=out_specs, check_vma=False
    )
```

profile of v0, /device:TPU:0, one launch (start us, length us, event | category | flops | bytes accessed | tf_op | source)
XLA Modules:
  0.0 565.7 jit_solution(10746559154888008046)
XLA Ops:
  9.3 7.0 %gather_fusion = bf16[512,7168]{1,0:T(8,128)(2,1)} fusion(bf16[65,7168]{1,0:T(8,128)(2,1)S(1)} %concatenate.6, s32[1024]{0:T(1024)S(1)} %pad_clamp_fusion.1), kind=kCustom, calls=%fused_computation | custom fusion | bytes 14682112 | tf_op jit(solution)/shard_map/gather | solution.py:92
  16.3 12.7 %reshape.71 = bf16[32,4,4,7168]{3,2,1,0:T(4,128)(2,1)} reshape(bf16[512,7168]{1,0:T(8,128)(2,1)} %gather_fusion) | data formatting | bytes 14680064 | tf_op jit(solution)/shard_map/reshape | solution.py:114
  29.0 7.5 %all-to-all-start = ((bf16[32,4,4,7168]{3,2,1,0:T(4,128)(2,1)}), bf16[32,4,4,7168]{3,2,1,0:T(4,128)(2,1)}, u32[]{:S(2)}, u32[]{:S(2)}) async-start(bf16[32,4,4,7168]{3,2,1,0:T(4,128)(2,1)} %reshape.71), calls=%async_computation | async-start | bytes 14680064 | tf_op jit(solution)/shard_map/all_to_all | solution.py:117
  36.5 91.9 %all-to-all-done = bf16[32,4,4,7168]{3,2,1,0:T(4,128)(2,1)} async-done(((bf16[32,4,4,7168]{3,2,1,0:T(4,128)(2,1)}), bf16[32,4,4,7168]{3,2,1,0:T(4,128)(2,1)}, u32[]{:S(2)}, u32[]{:S(2)}) %all-to-all-start) | async-done | bytes 7340064 | tf_op jit(solution)/shard_map/all_to_all | solution.py:117
  128.5 8.8 %copy.34 = bf16[1,4,32,4,7168]{4,3,2,1,0:T(4,128)(2,1)} copy(bf16[1,4,32,4,7168]{4,3,1,2,0:T(4,128)(2,1)} %bitcast.6) | data formatting | bytes 14680064 | tf_op jit(solution)/shard_map/all_to_all | solution.py:117
  137.3 12.1 %reshape.72 = bf16[4,128,7168]{2,1,0:T(8,128)(2,1)} reshape(bf16[1,4,32,4,7168]{4,3,2,1,0:T(4,128)(2,1)} %copy.34) | data formatting | bytes 14680064 | tf_op jit(solution)/shard_map/reshape | solution.py:118
  149.4 253.5 %while.13 = (s32[]{:T(128)}, bf16[4,128,7168]{2,1,0:T(8,128)(2,1)}, bf16[4,128,7168]{2,1,0:T(8,128)(2,1)}, s32[4]{0:T(128)S(1)}, s32[]{:T(128)}, /*index=5*/s32[1]{0:T(128)}) while((s32[]{:T(128)}, bf16[4,128,7168]{2,1,0:T(8,128)(2,1)}, bf16[4,128,7168]{2,1,0:T(8,128)(2,1)}, s32[4]{0:T(128)S(1)}, s32[]{:T(128)}, /*index=5*/s32[1]{0:T(128)}) %tuple.33), condition=%wide.region_7.8_spmd, body=%wide.region_6.7_spmd.sunk | while | flops 6035218432 | bytes 7175261 | solution.py:53
  150.9 20.1 %fusion.112 = f32[128,1024]{1,0:T(8,128)S(1)} fusion(s32[]{:T(128)} %bitcast.46, s32[7168]{0:T(1024)S(1)} %iota_multiply_fusion.4, bf16[4,128,7168]{2,1,0:T(8,128)(2,1)} %get-tuple-element.123, s32[]{:T(128)} %get-tuple-element.115), kind=kOutput, calls=%fused_computation.39.clone.1 | convolution fusion | flops 2011168768 | bytes 2388992 | tf_op jit(solution)/shard_map/while/body/eval_jaxpr/dot_general | solution.py:41
  171.0 20.1 %fusion.113 = bf16[128,1024]{1,0:T(8,128)(2,1)S(1)} fusion(s32[]{:T(128)} %bitcast.46, s32[7168]{0:T(1024)S(1)} %iota_multiply_fusion.4, bf16[4,128,7168]{2,1,0:T(8,128)(2,1)} %get-tuple-element.123, s32[]{:T(128)} %get-tuple-element.115, f32[128,1024]{1,0:T(8,128)S(1)} %fusion.112), kind=kOutput, calls=%fused_computation.48.clone.1 | convolution fusion | flops 2011955200 | bytes 2651136 | tf_op jit(solution)/shard_map/while/body/eval_jaxpr/dot_general | solution.py:42
  191.1 20.5 %fusion.114 = bf16[4,128,7168]{2,1,0:T(8,128)(2,1)} fusion(bf16[4,128,7168]{2,1,0:T(8,128)(2,1)} %get-tuple-element.116, s32[]{:T(128)} %get-tuple-element.115, bf16[128,1024]{1,0:T(8,128)(2,1)S(1)} %fusion.113, s32[]{:T(128)} %bitcast.46, s32[1024]{0:T(1024)S(1)} %iota_multiply_fusion.5), kind=kOutput, calls=%fused_computation.42.clone.1 | convolution fusion | flops 2012086272 | bytes 2102272 | tf_op jit(solution)/shard_map/while/body/eval_jaxpr/dot_general | solution.py:44
  213.1 19.9 %fusion.112 = f32[128,1024]{1,0:T(8,128)S(1)} fusion(s32[]{:T(128)} %bitcast.46, s32[7168]{0:T(1024)S(1)} %iota_multiply_fusion.4, bf16[4,128,7168]{2,1,0:T(8,128)(2,1)} %get-tuple-element.123, s32[]{:T(128)} %get-tuple-element.115), kind=kOutput, calls=%fused_computation.39.clone.1 | convolution fusion | flops 2011168768 | bytes 2388992 | tf_op jit(solution)/shard_map/while/body/eval_jaxpr/dot_general | solution.py:41
  233.0 20.3 %fusion.113 = bf16[128,1024]{1,0:T(8,128)(2,1)S(1)} fusion(s32[]{:T(128)} %bitcast.46, s32[7168]{0:T(1024)S(1)} %iota_multiply_fusion.4, bf16[4,128,7168]{2,1,0:T(8,128)(2,1)} %get-tuple-element.123, s32[]{:T(128)} %get-tuple-element.115, f32[128,1024]{1,0:T(8,128)S(1)} %fusion.112), kind=kOutput, calls=%fused_computation.48.clone.1 | convolution fusion | flops 2011955200 | bytes 2651136 | tf_op jit(solution)/shard_map/while/body/eval_jaxpr/dot_general | solution.py:42
  253.3 20.2 %fusion.114 = bf16[4,128,7168]{2,1,0:T(8,128)(2,1)} fusion(bf16[4,128,7168]{2,1,0:T(8,128)(2,1)} %get-tuple-element.116, s32[]{:T(128)} %get-tuple-element.115, bf16[128,1024]{1,0:T(8,128)(2,1)S(1)} %fusion.113, s32[]{:T(128)} %bitcast.46, s32[1024]{0:T(1024)S(1)} %iota_multiply_fusion.5), kind=kOutput, calls=%fused_computation.42.clone.1 | convolution fusion | flops 2012086272 | bytes 2102272 | tf_op jit(solution)/shard_map/while/body/eval_jaxpr/dot_general | solution.py:44
  275.2 19.9 %fusion.112 = f32[128,1024]{1,0:T(8,128)S(1)} fusion(s32[]{:T(128)} %bitcast.46, s32[7168]{0:T(1024)S(1)} %iota_multiply_fusion.4, bf16[4,128,7168]{2,1,0:T(8,128)(2,1)} %get-tuple-element.123, s32[]{:T(128)} %get-tuple-element.115), kind=kOutput, calls=%fused_computation.39.clone.1 | convolution fusion | flops 2011168768 | bytes 2388992 | tf_op jit(solution)/shard_map/while/body/eval_jaxpr/dot_general | solution.py:41
  295.1 20.4 %fusion.113 = bf16[128,1024]{1,0:T(8,128)(2,1)S(1)} fusion(s32[]{:T(128)} %bitcast.46, s32[7168]{0:T(1024)S(1)} %iota_multiply_fusion.4, bf16[4,128,7168]{2,1,0:T(8,128)(2,1)} %get-tuple-element.123, s32[]{:T(128)} %get-tuple-element.115, f32[128,1024]{1,0:T(8,128)S(1)} %fusion.112), kind=kOutput, calls=%fused_computation.48.clone.1 | convolution fusion | flops 2011955200 | bytes 2651136 | tf_op jit(solution)/shard_map/while/body/eval_jaxpr/dot_general | solution.py:42
  315.5 20.2 %fusion.114 = bf16[4,128,7168]{2,1,0:T(8,128)(2,1)} fusion(bf16[4,128,7168]{2,1,0:T(8,128)(2,1)} %get-tuple-element.116, s32[]{:T(128)} %get-tuple-element.115, bf16[128,1024]{1,0:T(8,128)(2,1)S(1)} %fusion.113, s32[]{:T(128)} %bitcast.46, s32[1024]{0:T(1024)S(1)} %iota_multiply_fusion.5), kind=kOutput, calls=%fused_computation.42.clone.1 | convolution fusion | flops 2012086272 | bytes 2102272 | tf_op jit(solution)/shard_map/while/body/eval_jaxpr/dot_general | solution.py:44
  337.2 20.1 %fusion.112 = f32[128,1024]{1,0:T(8,128)S(1)} fusion(s32[]{:T(128)} %bitcast.46, s32[7168]{0:T(1024)S(1)} %iota_multiply_fusion.4, bf16[4,128,7168]{2,1,0:T(8,128)(2,1)} %get-tuple-element.123, s32[]{:T(128)} %get-tuple-element.115), kind=kOutput, calls=%fused_computation.39.clone.1 | convolution fusion | flops 2011168768 | bytes 2388992 | tf_op jit(solution)/shard_map/while/body/eval_jaxpr/dot_general | solution.py:41
  357.3 20.1 %fusion.113 = bf16[128,1024]{1,0:T(8,128)(2,1)S(1)} fusion(s32[]{:T(128)} %bitcast.46, s32[7168]{0:T(1024)S(1)} %iota_multiply_fusion.4, bf16[4,128,7168]{2,1,0:T(8,128)(2,1)} %get-tuple-element.123, s32[]{:T(128)} %get-tuple-element.115, f32[128,1024]{1,0:T(8,128)S(1)} %fusion.112), kind=kOutput, calls=%fused_computation.48.clone.1 | convolution fusion | flops 2011955200 | bytes 2651136 | tf_op jit(solution)/shard_map/while/body/eval_jaxpr/dot_general | solution.py:42
  377.4 20.4 %fusion.114 = bf16[4,128,7168]{2,1,0:T(8,128)(2,1)} fusion(bf16[4,128,7168]{2,1,0:T(8,128)(2,1)} %get-tuple-element.116, s32[]{:T(128)} %get-tuple-element.115, bf16[128,1024]{1,0:T(8,128)(2,1)S(1)} %fusion.113, s32[]{:T(128)} %bitcast.46, s32[1024]{0:T(1024)S(1)} %iota_multiply_fusion.5), kind=kOutput, calls=%fused_computation.42.clone.1 | convolution fusion | flops 2012086272 | bytes 2102272 | tf_op jit(solution)/shard_map/while/body/eval_jaxpr/dot_general | solution.py:44
  402.9 11.7 %copy.44 = bf16[4,128,7168]{2,0,1:T(4,128)(2,1)} copy(bf16[4,128,7168]{2,1,0:T(8,128)(2,1)} %get-tuple-element.73) | data formatting | bytes 14680064 | tf_op jit(solution)/shard_map/while | solution.py:53
  420.3 91.5 %all-to-all-done.1 = bf16[1,4,128,7168]{3,1,0,2:T(4,128)(2,1)} async-done(((bf16[1,4,128,7168]{3,1,0,2:T(4,128)(2,1)}), bf16[1,4,128,7168]{3,1,0,2:T(4,128)(2,1)}, u32[]{:S(2)}, u32[]{:S(2)}) %all-to-all-start.1) | async-done | bytes 7340064 | tf_op jit(solution)/shard_map/all_to_all | solution.py:119
  511.8 9.9 %copy.43 = bf16[1,4,32,4,7168]{4,3,1,2,0:T(4,128)(2,1)} copy(bf16[1,4,32,4,7168]{4,1,3,2,0:T(4,128)(2,1)} %bitcast.8) | data formatting | bytes 14680064 | tf_op jit(solution)/shard_map/all_to_all | solution.py:119
  521.7 12.1 %reshape.74 = bf16[512,7168]{1,0:T(8,128)(2,1)} reshape(bf16[32,1,4,4,7168]{4,3,2,0,1:T(4,128)(2,1)} %bitcast.48) | data formatting | bytes 14680064 | tf_op jit(solution)/shard_map/reshape | solution.py:126
  540.6 18.2 %gather_fusion.1 = bf16[512,7168]{1,0:T(8,128)(2,1)} fusion(bf16[513,7168]{1,0:T(8,128)(2,1)} %concatenate.7, s32[1024]{0:T(1024)S(1)} %pad_clamp_fusion), kind=kCustom, calls=%fused_computation.1 | custom fusion | bytes 14682112 | tf_op jit(solution)/shard_map/gather | solution.py:97
  (52 shorter events, 30.6 us)
Async XLA Ops:
  2.2 5.8 %copy-start.1 = (pred[64,8]{0,1:T(8,128)(4,1)}, pred[64,8]{0,1:T(8,128)(4,1)S(1)}, u32[]{:S(2)}) copy-start(pred[64,8]{0,1:T(8,128)(4,1)S(1)} %compare_reduce_fusion) | copy-start | bytes 1540
  29.0 99.5 %all-to-all-start = ((bf16[32,4,4,7168]{3,2,1,0:T(4,128)(2,1)}), bf16[32,4,4,7168]{3,2,1,0:T(4,128)(2,1)}, u32[]{:S(2)}, u32[]{:S(2)}) async-start(bf16[32,4,4,7168]{3,2,1,0:T(4,128)(2,1)} %reshape.71), calls=%async_computation | async-start | bytes 14680064 | tf_op jit(solution)/shard_map/all_to_all | solution.py:117
  137.3 12.1 %copy-start.4 = (s32[4]{0:T(128)S(1)}, s32[4]{0:T(128)}, u32[]{:S(2)}) copy-start(s32[4]{0:T(128)} %param.11) | copy-start | bytes 52
  414.6 5.3 copy-start
  414.6 5.5 copy-start.3
  414.6 5.5 copy-start.2
  414.6 97.2 %all-to-all-start.1 = ((bf16[1,4,128,7168]{3,1,0,2:T(4,128)(2,1)}), bf16[1,4,128,7168]{3,1,0,2:T(4,128)(2,1)}, u32[]{:S(2)}, u32[]{:S(2)}) async-start(bf16[1,4,128,7168]{3,1,0,2:T(4,128)(2,1)} %bitcast.47), calls=%async_computation.1 | async-start | bytes 14680064 | tf_op jit(solution)/shard_map/all_to_all | solution.py:119
where the time goes:
time: 574 us; the launch traced here: 566 us
  matrix products  247 us (43%)
  waiting for transfers between devices  183 us (32%)
  local copies, waits for them, and re-layouts  108 us (19%)
  starting transfers between devices  12.8 us (2%)
  loops' own time  8.7 us (2%)
    all_to_all x1, waiting for transfers between devices, on_device(): lax.all_to_all(send_rows, ('node', 'local'), split_axis=0, concat_axis=2,...  91.9 us
    all_to_all x1, waiting for transfers between devices, on_device(): lax.all_to_all(results.reshape(1, EXP_DEV, -1, width), ('node', 'local'),...  91.5 us
    dot_general x4, matrix products, expert_block(): jnp.dot(hidden, weight_down, preferred_element_type=jnp.float32)  81.3 us
    dot_general x4, matrix products, expert_block(): up_part = jnp.dot(block_rows, weight_up, preferred_element_type=jnp.float32)  80.9 us
    dot_general x4, matrix products, expert_block(): jnp.dot(block_rows, weight_gate, preferred_element_type=jnp.float32)  80 us
    gather x1, local copies, waits for them, and re-layouts, combine_rows(): picked = padded[slot_index]  18.2 us
    reshape x1, local copies, waits for them, and re-layouts, on_device(): fill_slots(tokens, slot_index, slot_total)  12.7 us
    reshape x1, local copies, waits for them, and re-layouts, on_device(): returned.reshape(slot_total, width)  12.1 us
  transfers between devices with their start and end apart: 2, of which 2 were waited for; matrix products, arithmetic and copies ran while one was open for 0% of the time, Pallas kernels for 0%

commit v1 on v0

--- a/solution.py
+++ b/solution.py
@@ -101,31 +101,27 @@
 def on_device(tokens, expert_ids, node_groups, gate_levels, expert_seeds):
     tok_count = tokens.shape[0]
     width = tokens.shape[1]
-    devices_all = lax.axis_size(("node", "local"))
+    axes = ("rep", "node", "local")
+    rep_count = lax.axis_size("rep")
+    plane_count = lax.axis_size(("node", "local"))
     local_count = lax.axis_size("local")
-    experts_total = EXP_DEV * devices_all
+    seeds_here = expert_seeds.shape[0]
+    assert seeds_here == rep_count
+    experts_total = seeds_here * plane_count
     capacity = max(2, tok_count * TOP // experts_total)
-    group_size = EXP_DEV * local_count
+    group_size = seeds_here * local_count
     in_group = group_mask(expert_ids, node_groups, group_size)
     gate_share = gate_of(gate_levels, in_group)
     slot_rank, kept_mask = rank_of(expert_ids, in_group, 1, capacity, experts_total)
+    dest = (expert_ids % seeds_here) * plane_count + expert_ids // seeds_here
     slot_total = experts_total * capacity
-    slot_index = jnp.where(kept_mask, expert_ids * capacity + slot_rank, slot_total)
-    send_rows = fill_slots(tokens, slot_index, slot_total).reshape(
-        devices_all, EXP_DEV, capacity, width
-    )
-    arrived = lax.all_to_all(send_rows, ("node", "local"), split_axis=0, concat_axis=2, tiled=True)
-    results = run_experts(arrived.reshape(EXP_DEV, -1, width), expert_seeds)
-    returned = lax.all_to_all(
-        results.reshape(1, EXP_DEV, -1, width),
-        ("node", "local"),
-        split_axis=2,
-        concat_axis=0,
-        tiled=True,
-    )
-    return combine_rows(returned.reshape(slot_total, width), slot_index, gate_share).astype(
-        jnp.bfloat16
-    )
+    slot_index = jnp.where(kept_mask, dest * capacity + slot_rank, slot_total)
+    send_rows = fill_slots(tokens, slot_index, slot_total)
+    arrived = lax.all_to_all(send_rows, axes, split_axis=0, concat_axis=0, tiled=True)
+    my_seed = expert_seeds[lax.axis_index("rep")]
+    results = expert_block(arrived, my_seed)
+    returned = lax.all_to_all(results, axes, split_axis=0, concat_axis=0, tiled=True)
+    return combine_rows(returned, slot_index, gate_share).astype(jnp.bfloat16)
 
 
 def solution(mesh):

time: 574 us -> 365 us (0.64)
  the two profiles are of different devices: /device:TPU:0 before, /device:TPU:2 now
where the time goes in v1:
time: 365 us; the launch traced here: 358 us
  waiting for transfers between devices  175 us (48%)
  local copies, waits for them, and re-layouts  88.9 us (24%)
  matrix products  70.2 us (19%)
  starting transfers between devices  18.2 us (5%)
  other arithmetic  4.36 us (1%)
    all_to_all x1, waiting for transfers between devices, on_device(): lax.all_to_all(results, axes, split_axis=0, concat_axis=0, tiled=True)  88 us
    all_to_all x1, waiting for transfers between devices, on_device(): lax.all_to_all(send_rows, axes, split_axis=0, concat_axis=0, tiled=True)  86.9 us
    all_to_all x2, local copies, waits for them, and re-layouts, on_device(): lax.all_to_all(send_rows, axes, split_axis=0, concat_axis=0, tiled=True)  25.2 us
    all_to_all x2, local copies, waits for them, and re-layouts, on_device(): lax.all_to_all(results, axes, split_axis=0, concat_axis=0, tiled=True)  24.9 us
    dot_general x1, matrix products, expert_block(): jnp.dot(block_rows, weight_gate, preferred_element_type=jnp.float32)  22.5 us
    dot_general x1, matrix products, expert_block(): jnp.dot(hidden, weight_down, preferred_element_type=jnp.float32)  22.4 us
    dot_general x1, matrix products, expert_block(): up_part = jnp.dot(block_rows, weight_up, preferred_element_type=jnp.float32)  20.2 us
    gather x1, local copies, waits for them, and re-layouts, combine_rows(): picked = padded[slot_index]  17.9 us
  transfers between devices with their start and end apart: 2, of which 2 were waited for; matrix products, arithmetic and copies ran while one was open for 0% of the time, Pallas kernels for 0%

profile of v1, /device:TPU:2, one launch (start us, length us, event | category | flops | bytes accessed | tf_op | source)
XLA Modules:
  0.0 357.7 jit_solution(8760646328432952614)
XLA Ops:
  0.0 0.7 add_select_fusion.2
  0.7 0.8 copy.16
  1.5 0.7 compare_reduce_fusion
  2.6 1.3 select_reduce_fusion
  4.0 1.3 compare_select_fusion.1
  5.5 2.4 scatter_custom_fusion
  8.0 1.2 concatenate.6
  9.3 7.0 %gather_fusion = bf16[512,7168]{1,0:T(8,128)(2,1)} fusion(bf16[65,7168]{1,0:T(8,128)(2,1)S(1)} %concatenate.6, s32[1024]{0:T(1024)S(1)} %pad_clamp_fusion.1), kind=kCustom, calls=%fused_computation | custom fusion | bytes 14682112 | tf_op jit(solution)/shard_map/gather | solution.py:92
  16.3 12.6 %all_to_all.16 = bf16[128,4,7168]{2,1,0:T(4,128)(2,1)} reshape(bf16[512,7168]{1,0:T(8,128)(2,1)} %gather_fusion) | data formatting | bytes 14680064 | tf_op jit(solution)/shard_map/all_to_all | solution.py:120
  29.0 10.9 %all-to-all-start = ((bf16[128,4,7168]{2,1,0:T(4,128)(2,1)}), bf16[128,4,7168]{2,1,0:T(4,128)(2,1)}, u32[]{:S(2)}, u32[]{:S(2)}) async-start(bf16[128,4,7168]{2,1,0:T(4,128)(2,1)} %all_to_all.16), calls=%async_computation | async-start | bytes 14680064 | tf_op jit(solution)/shard_map/all_to_all | solution.py:120
  39.9 0.7 dynamic_slice.3
  41.3 86.9 %all-to-all-done = bf16[128,4,7168]{2,1,0:T(4,128)(2,1)} async-done(((bf16[128,4,7168]{2,1,0:T(4,128)(2,1)}), bf16[128,4,7168]{2,1,0:T(4,128)(2,1)}, u32[]{:S(2)}, u32[]{:S(2)}) %all-to-all-start) | async-done | bytes 7340064 | tf_op jit(solution)/shard_map/all_to_all | solution.py:120
  128.3 12.5 %all_to_all.18 = bf16[512,7168]{1,0:T(8,128)(2,1)} reshape(bf16[128,4,7168]{2,1,0:T(4,128)(2,1)} %all-to-all-done) | data formatting | bytes 14680064 | tf_op jit(solution)/shard_map/all_to_all | solution.py:120
  140.8 22.5 %fusion.41 = f32[512,1024]{1,0:T(8,128)S(1)} fusion(bf16[512,7168]{1,0:T(8,128)(2,1)} %all_to_all.18, s32[]{:T(128)} %bitcast.2, s32[7168]{0:T(1024)S(1)} %iota_multiply_fusion), kind=kOutput, calls=%fused_computation.52 | convolution fusion | flops 7648313344 | bytes 9465860 | tf_op jit(solution)/shard_map/dot_general | solution.py:41
  163.3 20.2 %multiply_convert_fusion = bf16[512,1024]{1,0:T(8,128)(2,1)S(1)} fusion(f32[512,1024]{1,0:T(8,128)S(1)} %fusion.41, bf16[512,7168]{1,0:T(8,128)(2,1)S(1)} %copy-done, s32[]{:T(128)} %bitcast.2, s32[7168]{0:T(1024)S(1)} %iota_multiply_fusion), kind=kOutput, calls=%fused_computation.56 | convolution fusion | flops 7651459072 | bytes 10514436 | tf_op jit(solution)/shard_map/dot_general | solution.py:42
  183.5 22.4 %fusion.43 = bf16[512,7168]{1,0:T(8,128)(2,1)} fusion(bf16[512,1024]{1,0:T(8,128)(2,1)S(1)} %multiply_convert_fusion, s32[]{:T(128)} %bitcast.2, s32[1024]{0:T(1024)S(1)} %iota_multiply_fusion.1), kind=kOutput, calls=%fused_computation.53 | convolution fusion | flops 7651983360 | bytes 8392708 | tf_op jit(solution)/shard_map/dot_general | solution.py:44
  205.9 12.8 %all_to_all.19 = bf16[128,4,7168]{2,1,0:T(4,128)(2,1)} reshape(bf16[512,7168]{1,0:T(8,128)(2,1)} %fusion.43) | data formatting | bytes 14680064 | tf_op jit(solution)/shard_map/all_to_all | solution.py:123
  218.7 7.3 %all-to-all-start.1 = ((bf16[128,4,7168]{2,1,0:T(4,128)(2,1)}), bf16[128,4,7168]{2,1,0:T(4,128)(2,1)}, u32[]{:S(2)}, u32[]{:S(2)}) async-start(bf16[128,4,7168]{2,1,0:T(4,128)(2,1)} %all_to_all.19), calls=%async_computation.1 | async-start | bytes 14680064 | tf_op jit(solution)/shard_map/all_to_all | solution.py:123
  226.3 88.0 %all-to-all-done.1 = bf16[128,4,7168]{2,1,0:T(4,128)(2,1)} async-done(((bf16[128,4,7168]{2,1,0:T(4,128)(2,1)}), bf16[128,4,7168]{2,1,0:T(4,128)(2,1)}, u32[]{:S(2)}, u32[]{:S(2)}) %all-to-all-start.1) | async-done | bytes 7340064 | tf_op jit(solution)/shard_map/all_to_all | solution.py:123
  314.3 12.1 %all_to_all.21 = bf16[512,7168]{1,0:T(8,128)(2,1)} reshape(bf16[128,4,7168]{2,1,0:T(4,128)(2,1)} %all-to-all-done.1) | data formatting | bytes 14680064 | tf_op jit(solution)/shard_map/all_to_all | solution.py:123
  326.4 6.8 %concatenate.7 = bf16[513,7168]{1,0:T(8,128)(2,1)} pad(bf16[512,7168]{1,0:T(8,128)(2,1)} %all_to_all.21, bf16[]{:T(256)} %constant.45.clone.1), padding=0_1x0_0 | pad | bytes 14694402 | tf_op jit(solution)/shard_map/concatenate | solution.py:96
  333.2 17.9 %gather_fusion.1 = bf16[512,7168]{1,0:T(8,128)(2,1)} fusion(bf16[513,7168]{1,0:T(8,128)(2,1)} %concatenate.7, s32[1024]{0:T(1024)S(1)} %pad_clamp_fusion), kind=kCustom, calls=%fused_computation.1 | custom fusion | bytes 14682112 | tf_op jit(solution)/shard_map/gather | solution.py:97
  351.1 5.1 %fusion.46 = bf16[64,1,7168]{2,1,0:T(2,128)(2,1)S(1)} fusion(bf16[64,8,1]{1,2,0:T(2,128)(2,1)S(1)} %copy.22, bf16[512,7168]{1,0:T(8,128)(2,1)} %gather_fusion.1), kind=kOutput, calls=%fused_computation.54 | convolution fusion | flops 7340032 | bytes 8258560 | tf_op jit(solution)/shard_map/tj,tjd->td/dot_general | solution.py:98
  356.3 1.2 copy.25
  (32 shorter events, 1.1 us)
Async XLA Ops:
  2.2 5.9 %copy-start.2 = (pred[64,8]{0,1:T(8,128)(4,1)}, pred[64,8]{0,1:T(8,128)(4,1)S(1)}, u32[]{:S(2)}) copy-start(pred[64,8]{0,1:T(8,128)(4,1)S(1)} %compare_reduce_fusion) | copy-start | bytes 1540
  29.0 10.9 %copy-start.5 = (s32[4]{0:T(128)S(1)}, s32[4]{0:T(128)}, u32[]{:S(2)}) copy-start(s32[4]{0:T(128)} %param.9) | copy-start | bytes 52
  29.0 99.3 %all-to-all-start = ((bf16[128,4,7168]{2,1,0:T(4,128)(2,1)}), bf16[128,4,7168]{2,1,0:T(4,128)(2,1)}, u32[]{:S(2)}, u32[]{:S(2)}) async-start(bf16[128,4,7168]{2,1,0:T(4,128)(2,1)} %all_to_all.16), calls=%async_computation | async-start | bytes 14680064 | tf_op jit(solution)/shard_map/all_to_all | solution.py:120
  140.8 22.5 %copy-start = (bf16[512,7168]{1,0:T(8,128)(2,1)S(1)}, bf16[512,7168]{1,0:T(8,128)(2,1)}, u32[]{:S(2)}) copy-start(bf16[512,7168]{1,0:T(8,128)(2,1)} %all_to_all.18) | copy-start | bytes 22020100
  218.7 7.3 %copy-start.1 = (s32[64,8]{0,1:T(8,128)S(1)}, s32[64,8]{0,1:T(8,128)}, u32[]{:S(2)}) copy-start(s32[64,8]{0,1:T(8,128)} %get-tuple-element.5) | copy-start | bytes 6148
  218.7 7.5 %copy-start.4 = (s32[64,8]{0,1:T(8,128)S(1)}, s32[64,8]{0,1:T(8,128)}, u32[]{:S(2)}) copy-start(s32[64,8]{0,1:T(8,128)} %param.8) | copy-start | bytes 6148
  218.7 7.5 %copy-start.3 = (pred[64,8]{0,1:T(8,128)(4,1)S(1)}, pred[64,8]{0,1:T(8,128)(4,1)}, u32[]{:S(2)}) copy-start(pred[64,8]{0,1:T(8,128)(4,1)} %copy-done.2) | copy-start | bytes 1540
  218.7 95.6 %all-to-all-start.1 = ((bf16[128,4,7168]{2,1,0:T(4,128)(2,1)}), bf16[128,4,7168]{2,1,0:T(4,128)(2,1)}, u32[]{:S(2)}, u32[]{:S(2)}) async-start(bf16[128,4,7168]{2,1,0:T(4,128)(2,1)} %all_to_all.19), calls=%async_computation.1 | async-start | bytes 14680064 | tf_op jit(solution)/shard_map/all_to_all | solution.py:123

commit v2 on v1

--- a/solution.py
+++ b/solution.py
@@ -98,6 +98,23 @@
     return jnp.einsum("tj,tjd->td", gate_share, picked.astype(jnp.float32))
 
 
+def expert_weights(expert_seed):
+    weight_gate = hashed_weight(expert_seed, salt_gate, D, FF, D)
+    weight_up = hashed_weight(expert_seed, salt_up, D, FF, D)
+    weight_down = hashed_weight(expert_seed, salt_down, FF, D, FF)
+    return lax.optimization_barrier((weight_gate, weight_up, weight_down))
+
+
+def expert_rows(block_rows, weights):
+    weight_gate, weight_up, weight_down = weights
+    gate_part = jnp.einsum("sct,tf->scf", block_rows, weight_gate, preferred_element_type=jnp.float32)
+    up_part = jnp.einsum("sct,tf->scf", block_rows, weight_up, preferred_element_type=jnp.float32)
+    hidden = (jax.nn.silu(gate_part) * up_part).astype(jnp.bfloat16)
+    return jnp.einsum("scf,ft->sct", hidden, weight_down, preferred_element_type=jnp.float32).astype(
+        jnp.bfloat16
+    )
+
+
 def on_device(tokens, expert_ids, node_groups, gate_levels, expert_seeds):
     tok_count = tokens.shape[0]
     width = tokens.shape[1]
@@ -108,6 +125,7 @@
     seeds_here = expert_seeds.shape[0]
     assert seeds_here == rep_count
     experts_total = seeds_here * plane_count
+    devices_all = experts_total
     capacity = max(2, tok_count * TOP // experts_total)
     group_size = seeds_here * local_count
     in_group = group_mask(expert_ids, node_groups, group_size)
@@ -116,12 +134,23 @@
     dest = (expert_ids % seeds_here) * plane_count + expert_ids // seeds_here
     slot_total = experts_total * capacity
     slot_index = jnp.where(kept_mask, dest * capacity + slot_rank, slot_total)
-    send_rows = fill_slots(tokens, slot_index, slot_total)
+    token_index = lax.broadcasted_iota(jnp.int32, slot_index.shape, 0)
+    slot_token = (
+        jnp.full((slot_total,), tok_count, jnp.int32)
+        .at[slot_index.reshape(-1)]
+        .set(token_index.reshape(-1), mode="drop")
+    )
+    padded = jnp.concatenate([tokens, jnp.zeros((1, width), tokens.dtype)], axis=0)
+    send_rows = padded[slot_token.reshape(devices_all, capacity)]
+    weights = expert_weights(expert_seeds[lax.axis_index("rep")])
     arrived = lax.all_to_all(send_rows, axes, split_axis=0, concat_axis=0, tiled=True)
-    my_seed = expert_seeds[lax.axis_index("rep")]
-    results = expert_block(arrived, my_seed)
+    results = expert_rows(arrived, weights)
     returned = lax.all_to_all(results, axes, split_axis=0, concat_axis=0, tiled=True)
-    return combine_rows(returned, slot_index, gate_share).astype(jnp.bfloat16)
+    safe_dest = jnp.where(kept_mask, dest, 0)
+    safe_rank = jnp.where(kept_mask, slot_rank, 0)
+    picked = returned[safe_dest, safe_rank]
+    share = jnp.where(kept_mask, gate_share, 0.0)
+    return jnp.einsum("tj,tjd->td", share, picked.astype(jnp.float32)).astype(jnp.bfloat16)
 
 
 def solution(mesh):

time: 365 us -> 312 us (0.85); the launches traced: 358 us -> 311 us
  waiting for transfers between devices: 175 us -> 120 us
  other arithmetic: 4.36 us -> 58.9 us
  matrix products: 70.2 us -> 42 us
  local copies, waits for them, and re-layouts: 88.9 us -> 70.9 us
    convert_element_type x0 -> x2, other arithmetic: none -> 55.1 us  [hashed_weight(): ((sixteen_bits - 32767.5) * (math.sqrt(3.0 / fan_in) / 32768.0)).astype(j...]
    all_to_all x1, waiting for transfers between devices: 86.9 us -> 32 us  [on_device(): lax.all_to_all(send_rows, axes, split_axis=0, concat_axis=0, tiled=True)]
    all_to_all x4 -> x0, local copies, waits for them, and re-layouts: 50 us -> none  [the longest x2 25.2 us: on_device(): lax.all_to_all(send_rows, axes, split_axis=0, concat_axis=0, tiled=True)]
    dot_general x4, matrix products: 70.2 us -> 42 us  [the longest x1 13.7 us: expert_rows(): jnp.einsum('sct,tf->scf', block_rows, weight_up, preferred_element_type=j...]
    gather x2 -> x3, local copies, waits for them, and re-layouts: 25 us -> 51.9 us  [the longest x1 32.2 us: on_device(): picked = returned[safe_dest, safe_rank]]
    convert_element_type x0 -> x1, local copies, waits for them, and re-layouts: none -> 11.8 us  [expert_rows(): jnp.einsum('scf,ft->sct', hidden, weight_down, preferred_element_type=jnp...]
    concatenate x2 -> x3, local copies, waits for them, and re-layouts: 8.08 us -> 1.43 us  [the longest x1 1.25 us: on_device(): jnp.concatenate([tokens, jnp.zeros((1, width), tokens.dtype)], axis=0)]
  transfers between devices with their start and end apart: 2 -> 2, of which waited for: 2 -> 2; matrix products, arithmetic and copies ran while one was open for 0% -> 18% of each run, Pallas kernels for 0% -> 0%
where the time goes in v2:
time: 312 us; the launch traced here: 311 us
  waiting for transfers between devices  120 us (38%)
  local copies, waits for them, and re-layouts  70.9 us (23%)
  other arithmetic  58.9 us (19%)
  matrix products  42 us (13%)
  starting transfers between devices  18.1 us (6%)
    all_to_all x1, waiting for transfers between devices, on_device(): lax.all_to_all(results, axes, split_axis=0, concat_axis=0, tiled=True)  88 us
    convert_element_type x2, other arithmetic, hashed_weight(): ((sixteen_bits - 32767.5) * (math.sqrt(3.0 / fan_in) / 32768.0)).astype(j...  55.1 us
    gather x1, local copies, waits for them, and re-layouts, on_device(): picked = returned[safe_dest, safe_rank]  32.2 us
    all_to_all x1, waiting for transfers between devices, on_device(): lax.all_to_all(send_rows, axes, split_axis=0, concat_axis=0, tiled=True)  32 us
    gather x2, local copies, waits for them, and re-layouts, on_device(): send_rows = padded[slot_token.reshape(devices_all, capacity)]  19.7 us
    dot_general x1, matrix products, expert_rows(): jnp.einsum('sct,tf->scf', block_rows, weight_up, preferred_element_type=j...  13.7 us
    dot_general x1, matrix products, expert_rows(): jnp.einsum('sct,tf->scf', block_rows, weight_gate, preferred_element_type...  13.3 us
    convert_element_type x1, local copies, waits for them, and re-layouts, expert_rows(): jnp.einsum('scf,ft->sct', hidden, weight_down, preferred_element_type=jnp...  11.8 us
  transfers between devices with their start and end apart: 2, of which 2 were waited for; matrix products, arithmetic and copies ran while one was open for 18% of the time, Pallas kernels for 0%

profile of v2, /device:TPU:2, one launch (start us, length us, event | category | flops | bytes accessed | tf_op | source)
XLA Modules:
  0.0 310.7 jit_solution(8989266018211766045)
XLA Ops:
  0.0 0.7 add_select_fusion.2
  0.7 0.8 copy.28
  1.5 0.7 compare_reduce_fusion
  2.3 0.2 convert_reduce_fusion
  2.6 1.3 select_reduce_fusion
  4.0 0.7 add_select_fusion.3
  5.0 2.4 scatter_custom_fusion
  7.6 1.2 concatenate.6
  8.9 7.0 %gather_fusion = bf16[512,7168]{1,0:T(8,128)(2,1)} fusion(bf16[65,7168]{1,0:T(8,128)(2,1)S(1)} %concatenate.6, s32[1024]{0:T(1024)S(1)} %pad_clamp_fusion), kind=kCustom, calls=%fused_computation | custom fusion | bytes 14682112 | tf_op jit(solution)/shard_map/gather | solution.py:144
  16.0 12.6 %reshape.116 = bf16[128,4,7168]{2,1,0:T(4,128)(2,1)} reshape(bf16[512,7168]{1,0:T(8,128)(2,1)} %gather_fusion) | data formatting | bytes 14680064 | tf_op jit(solution)/shard_map/gather | solution.py:144
  28.6 10.9 %all-to-all-start = ((bf16[128,4,7168]{2,1,0:T(4,128)(2,1)}), bf16[128,4,7168]{2,1,0:T(4,128)(2,1)}, u32[]{:S(2)}, u32[]{:S(2)}) async-start(bf16[128,4,7168]{2,1,0:T(4,128)(2,1)} %reshape.116), calls=%async_computation | async-start | bytes 14680064 | tf_op jit(solution)/shard_map/all_to_all | solution.py:146
  39.6 0.6 dynamic_slice.3
  40.8 18.7 %fusion.23 = bf16[1024,7168]{1,0:T(8,128)(2,1)} fusion(s32[]{:T(128)} %bitcast.2, s32[1024]{0:T(1024)S(1)} %iota_multiply_fusion.1), kind=kLoop, calls=%fused_computation.35 | loop fusion | flops 132120576 | bytes 14684164 | tf_op jit(solution)/shard_map/convert_element_type | solution.py:34
  59.5 36.4 %fusion.15 = (bf16[7168,1024]{1,0:T(8,128)(2,1)}, bf16[7168,1024]{1,0:T(8,128)(2,1)}) fusion(s32[]{:T(128)} %bitcast.2, s32[7168]{0:T(1024)S(1)} %iota_multiply_fusion), kind=kLoop, calls=%fused_computation.27 | loop fusion | flops 242221056 | bytes 29388804 | tf_op jit(solution)/shard_map/convert_element_type | solution.py:34
  95.9 32.0 %all-to-all-done = bf16[128,4,7168]{2,1,0:T(4,128)(2,1)} async-done(((bf16[128,4,7168]{2,1,0:T(4,128)(2,1)}), bf16[128,4,7168]{2,1,0:T(4,128)(2,1)}, u32[]{:S(2)}, u32[]{:S(2)}) %all-to-all-start) | async-done | bytes 7340064 | tf_op jit(solution)/shard_map/all_to_all | solution.py:146
  127.9 13.3 %fusion.28 = f32[128,4,1024]{2,0,1:T(8,128)S(1)} fusion(bf16[7168,1024]{1,0:T(8,128)(2,1)} %get-tuple-element.8, bf16[128,4,7168]{2,1,0:T(4,128)(2,1)} %all-to-all-done), kind=kOutput, calls=%fused_computation.41 | convolution fusion | flops 7516192768 | bytes 24117248 | tf_op jit(solution)/shard_map/sct,tf->scf/dot_general | solution.py:110
  141.2 13.7 %multiply_convert_fusion = bf16[128,4,1024]{2,0,1:T(8,128)(2,1)S(1)} fusion(f32[128,4,1024]{2,0,1:T(8,128)S(1)} %fusion.28, bf16[7168,1024]{1,0:T(8,128)(2,1)} %get-tuple-element.9, bf16[128,4,7168]{2,1,0:T(4,128)(2,1)} %all-to-all-done), kind=kOutput, calls=%fused_computation.48 | convolution fusion | flops 7519338496 | bytes 25165824 | tf_op jit(solution)/shard_map/sct,tf->scf/dot_general | solution.py:111
  155.0 9.9 %fusion.30 = bf16[128,4,7168]{2,0,1:T(8,128)(2,1)} fusion(bf16[128,4,1024]{2,0,1:T(8,128)(2,1)S(1)} %multiply_convert_fusion, bf16[1024,7168]{1,0:T(8,128)(2,1)S(1)} %bitcast.46), kind=kOutput, calls=%fused_computation.43 | convolution fusion | flops 7519862784 | bytes 23068672 | tf_op jit(solution)/shard_map/scf,ft->sct/dot_general | solution.py:113
  164.8 11.8 %copy.35 = bf16[128,4,7168]{2,1,0:T(4,128)(2,1)} copy(bf16[128,4,7168]{2,0,1:T(8,128)(2,1)} %fusion.30) | data formatting | bytes 14680064 | tf_op jit(solution)/shard_map/convert_element_type | solution.py:113
  176.6 7.1 %all-to-all-start.1 = ((bf16[128,4,7168]{2,1,0:T(4,128)(2,1)}), bf16[128,4,7168]{2,1,0:T(4,128)(2,1)}, u32[]{:S(2)}, u32[]{:S(2)}) async-start(bf16[128,4,7168]{2,1,0:T(4,128)(2,1)} %copy.35), calls=%async_computation.1 | async-start | bytes 14680064 | tf_op jit(solution)/shard_map/all_to_all | solution.py:148
  184.1 88.0 %all-to-all-done.1 = bf16[128,4,7168]{2,1,0:T(4,128)(2,1)} async-done(((bf16[128,4,7168]{2,1,0:T(4,128)(2,1)}), bf16[128,4,7168]{2,1,0:T(4,128)(2,1)}, u32[]{:S(2)}, u32[]{:S(2)}) %all-to-all-start.1) | async-done | bytes 7340064 | tf_op jit(solution)/shard_map/all_to_all | solution.py:148
  272.1 32.2 %gather_fusion.1 = bf16[512,7168]{1,0:T(8,128)(2,1)} fusion(bf16[128,4,7168]{2,1,0:T(4,128)(2,1)} %all-to-all-done.1, s32[512]{0:T(512)S(1)} %reshape.123), kind=kCustom, calls=%fused_computation.1 | custom fusion | bytes 14684160 | tf_op jit(solution)/shard_map/gather | solution.py:151
  304.4 5.1 %fusion.33 = bf16[64,1,7168]{2,1,0:T(2,128)(2,1)S(1)} fusion(bf16[64,8,1]{1,2,0:T(2,128)(2,1)S(1)} %copy.38, bf16[512,7168]{1,0:T(8,128)(2,1)} %gather_fusion.1), kind=kOutput, calls=%fused_computation.44 | convolution fusion | flops 7340032 | bytes 8258560 | tf_op jit(solution)/shard_map/tj,tjd->td/dot_general | solution.py:153
  309.5 1.2 copy.47
  (36 shorter events, 1.1 us)
Async XLA Ops:
  15.9 23.6 %copy-start.2 = (s32[4]{0:T(128)S(1)}, s32[4]{0:T(128)}, u32[]{:S(2)}) copy-start(s32[4]{0:T(128)} %param.9) | copy-start | bytes 52
  28.6 99.3 %all-to-all-start = ((bf16[128,4,7168]{2,1,0:T(4,128)(2,1)}), bf16[128,4,7168]{2,1,0:T(4,128)(2,1)}, u32[]{:S(2)}, u32[]{:S(2)}) async-start(bf16[128,4,7168]{2,1,0:T(4,128)(2,1)} %reshape.116), calls=%async_computation | async-start | bytes 14680064 | tf_op jit(solution)/shard_map/all_to_all | solution.py:146
  127.9 27.0 %slice-start = ((s8[14680064]{0:T(1024)(128)(4,1)}), s8[4194304]{0:T(1024)(128)(4,1)S(1)}, s32[]{:S(2)}) async-start(s8[14680064]{0:T(1024)(128)(4,1)} %bitcast.45), calls=%async_computation.2 | async-start | bytes 8388608
  127.9 27.0 %slice-start.1 = ((s8[14680064]{0:T(1024)(128)(4,1)}), s8[4194304]{0:T(1024)(128)(4,1)S(1)}, s32[]{:S(2)}) async-start(s8[14680064]{0:T(1024)(128)(4,1)} %bitcast.45), calls=%async_computation.3 | async-start | bytes 8388608
  127.9 27.0 %slice-start.2 = ((s8[14680064]{0:T(1024)(128)(4,1)}), s8[4194304]{0:T(1024)(128)(4,1)S(1)}, s32[]{:S(2)}) async-start(s8[14680064]{0:T(1024)(128)(4,1)} %bitcast.45), calls=%async_computation.4 | async-start | bytes 8388608
  141.2 13.7 %slice-start.3 = ((s8[14680064]{0:T(1024)(128)(4,1)}), s8[2097152]{0:T(1024)(128)(4,1)S(1)}, s32[]{:S(2)}) async-start(s8[14680064]{0:T(1024)(128)(4,1)} %bitcast.45), calls=%async_computation.5 | async-start | bytes 4194304
  164.8 19.0 %copy-start = (s32[64,8]{0,1:T(8,128)S(1)}, s32[64,8]{0,1:T(8,128)}, u32[]{:S(2)}) copy-start(s32[64,8]{0,1:T(8,128)} %param.6) | copy-start | bytes 6148
  164.8 19.2 %copy-start.1 = (s32[64,8]{0,1:T(8,128)S(1)}, s32[64,8]{0,1:T(8,128)}, u32[]{:S(2)}) copy-start(s32[64,8]{0,1:T(8,128)} %param.8) | copy-start | bytes 6148
  176.6 95.5 %all-to-all-start.1 = ((bf16[128,4,7168]{2,1,0:T(4,128)(2,1)}), bf16[128,4,7168]{2,1,0:T(4,128)(2,1)}, u32[]{:S(2)}, u32[]{:S(2)}) async-start(bf16[128,4,7168]{2,1,0:T(4,128)(2,1)} %copy.35), calls=%async_computation.1 | async-start | bytes 14680064 | tf_op jit(solution)/shard_map/all_to_all | solution.py:148
